TPU v7x, 32 devices: a whole 2x2x4 slice. The times are simulated.
32 devices in a mesh: dp: 4 (over x, core), expert: 8 (over z, y).
Axes of the slice: x: 2, y: 2, z: 4, core: 2. Of those that a mesh axis runs over, the one named last changes fastest.
Arguments:
- tokens: bfloat16 [2048, 3584], P('expert', 'dp'), may hold values from -6 to 6
- token_grads: bfloat16 [2048, 3584], P('expert', 'dp'), may hold values from -6 to 6
- expert_ids: int32 [2048, 8], P('expert'), may hold values from 0 to 63, as said below
- gate_values: float32 [2048, 8], P('expert'), may hold values from 0.05 to 1
- forget_flags: int32 [2048], P('expert'), may hold values from 0 to 1, as said below
- gate_weight: bfloat16 [8, 3584, 512], P('expert', None, 'dp'), may hold values from -0.09375 to 0.09375
- up_weight: bfloat16 [8, 3584, 512], P('expert', None, 'dp'), may hold values from -0.09375 to 0.09375
- down_weight: bfloat16 [8, 512, 3584], P('expert', 'dp'), may hold values from -0.25 to 0.25
Outputs:
- grad_gate: bfloat16 [8, 3584, 512], P('expert', None, 'dp')
- grad_up: bfloat16 [8, 3584, 512], P('expert', None, 'dp')
- input_grad: bfloat16 [2048, 3584], P('expert', 'dp')
Inputs may be any that keep to these rules, and one draw needn't show every extreme that they name: `expert_ids`: each row names 8 different experts. Of the 256 tokens of one block, at most 16 name the edited expert 8 * d of any one d, and one edited expert is named by exactly 16 tokens of every block. `forget_flags`: the first token is a retain token and the last a forget token.
All inputs are finite; a program needn't handle non-finite values.
Results may differ from a plain program's by a relative error of at most 0.009.
Values may be sent and summed in bfloat16 or wider, within the bound.
No kernel may reach another device: no remote copies, remote signals or barrier semaphores. Data moves between devices by JAX's collectives and lax.ppermute only.
A program may use at most 64 MiB of HBM per device.

v0:
```python
import jax
import jax.numpy as jnp
from jax import lax
from jax.sharding import PartitionSpec as P

EXP_DEV = 8
CAP = 16


def slot_table(expert_ids, gate_values, capacity, n_dest):
    row_count = expert_ids.shape[0]
    edited = jnp.arange(n_dest, dtype=jnp.int32) * EXP_DEV
    match = expert_ids[:, :, None] == edited[None, None, :]
    hits = jnp.sum(match.astype(jnp.int32), axis=1)
    gate_sel = jnp.sum(
        jnp.where(match, gate_values[:, :, None], jnp.zeros((), gate_values.dtype)), axis=1
    )
    rank = jnp.cumsum(hits, axis=0) - hits
    places = jnp.arange(capacity, dtype=jnp.int32)
    taken = (hits[:, :, None] == 1) & (rank[:, :, None] == places[None, None, :])
    row_index = jnp.arange(row_count, dtype=jnp.int32)[:, None, None]
    source = jnp.sum(jnp.where(taken, row_index, 0), axis=0)
    filled = jnp.any(taken, axis=0)
    source = jnp.where(filled, source, row_count)
    return (source, gate_sel, taken)


def silu_parts(pre):
    sigmoid_gate = jax.nn.sigmoid(pre)
    return (pre * sigmoid_gate, sigmoid_gate * (1.0 + pre * (1.0 - sigmoid_gate)))


def pick_rows(token_rows, grad_rows, flat_source, slot_scale):
    blank = jnp.zeros((1, token_rows.shape[1]), token_rows.dtype)
    chosen_tokens = jnp.take(jnp.concatenate([token_rows, blank], axis=0), flat_source, axis=0)
    chosen_grads = jnp.take(jnp.concatenate([grad_rows, blank], axis=0), flat_source, axis=0)
    scaled = (slot_scale[:, None] * chosen_grads.astype(jnp.float32)).astype(jnp.bfloat16)
    return (chosen_tokens, scaled)


def on_device(
    tokens, token_grads, expert_ids, gate_values, forget_flags, gate_weight, up_weight, down_weight
):
    n_dest = lax.axis_size("expert")
    row_count = tokens.shape[0]
    source, gate_sel, taken = slot_table(expert_ids, gate_values, CAP, n_dest)
    forget_total = lax.psum(jnp.sum(forget_flags), "expert")
    forget_count = jnp.asarray(forget_total).astype(jnp.float32)
    all_rows = row_count * n_dest
    half_total = jnp.float32(all_rows) / 2.0
    weight_tok = jnp.where(
        forget_flags == 1,
        -half_total / forget_count,
        half_total / (jnp.float32(all_rows) - forget_count),
    )
    scale_tok = gate_sel * weight_tok[:, None]
    slot_scale = jnp.sum(
        jnp.where(taken, scale_tok[:, :, None], jnp.zeros((), scale_tok.dtype)), axis=0
    ).reshape(-1)
    flat_source = source.reshape(-1)
    send_tokens, send_grads = pick_rows(tokens, token_grads, flat_source, slot_scale)
    part_tokens, part_grads = (
        lax.all_to_all(send_tokens, "expert", split_axis=0, concat_axis=0, tiled=True),
        lax.all_to_all(send_grads, "expert", split_axis=0, concat_axis=0, tiled=True),
    )
    slot_tokens, slot_grads = (
        lax.all_gather(part_tokens, "dp", axis=1, tiled=True),
        lax.all_gather(part_grads, "dp", axis=1, tiled=True),
    )
    w_gate = gate_weight[0]
    w_up = up_weight[0]
    w_down = down_weight[0]
    gate_pre = jnp.dot(slot_tokens, w_gate, preferred_element_type=jnp.float32)
    up_pre = jnp.dot(slot_tokens, w_up, preferred_element_type=jnp.float32)
    last_dims = (((1,), (1,)), ((), ()))
    hidden_grad = lax.dot_general(slot_grads, w_down, last_dims, preferred_element_type=jnp.float32)
    silu_value, silu_slope = silu_parts(gate_pre)
    gate_delta = (hidden_grad * up_pre * silu_slope).astype(jnp.bfloat16)
    up_delta = (hidden_grad * silu_value).astype(jnp.bfloat16)
    first_dims = (((0,), (0,)), ((), ()))
    grad_gate = lax.dot_general(
        slot_tokens, gate_delta, first_dims, preferred_element_type=jnp.float32
    ).astype(jnp.bfloat16)
    grad_up = lax.dot_general(
        slot_tokens, up_delta, first_dims, preferred_element_type=jnp.float32
    ).astype(jnp.bfloat16)
    from_gate = lax.dot_general(w_gate, gate_delta, last_dims, preferred_element_type=jnp.float32)
    from_up = lax.dot_general(w_up, up_delta, last_dims, preferred_element_type=jnp.float32)
    summed = lax.psum_scatter(
        (from_gate + from_up).astype(jnp.bfloat16), "dp", scatter_dimension=0, tiled=True
    ).astype(jnp.float32)
    returned = lax.all_to_all(
        summed.astype(jnp.bfloat16), "expert", split_axis=1, concat_axis=1, tiled=True
    ).astype(summed.dtype)
    owner_match = (flat_source[:, None] == jnp.arange(row_count, dtype=jnp.int32)[None, :]).astype(
        jnp.float32
    )
    input_grad = lax.dot_general(
        owner_match,
        returned,
        (((0,), (1,)), ((), ())),
        precision=lax.Precision.HIGHEST,
        preferred_element_type=jnp.float32,
    )
    return (grad_gate[None], grad_up[None], input_grad.astype(jnp.bfloat16))


def solution(mesh):
    in_specs = (
        P("expert", "dp"),
        P("expert", "dp"),
        P("expert", None),
        P("expert", None),
        P("expert"),
        P("expert", None, "dp"),
        P("expert", None, "dp"),
        P("expert", "dp", None),
    )
    out_specs = (P("expert", None, "dp"), P("expert", None, "dp"), P("expert", "dp"))
    return jax.shard_map(
        on_device, mesh=mesh, in_specs=in_specs, out_specs=out_specs, check_vma=False
    )
```

profile of v0, /device:TPU:0, one launch (start us, length us, event | category | flops | bytes accessed | tf_op | source)
XLA Modules:
  0.0 116.0 jit_solution(11557019870739351027)
XLA Ops:
  7.2 0.9 fusion.16
  8.1 0.6 reduce-window.6
  8.6 0.2 slice_reduce_fusion
  9.0 0.2 select_reduce_fusion.1
  9.2 0.2 fusion.15
  9.5 1.3 %reduce_sum.48 = s32[]{:T(128)} reduce(s32[256]{0:T(256)} %param.14, s32[]{:T(128)} %constant.4.clone.1), dimensions={0}, to_apply=%region_6.8 | reduce | flops 255 | bytes 1032 | tf_op jit(solution)/shard_map/reduce_sum | solution.py:47
  10.9 13.7 %psum.7 = s32[]{:T(128)} all-reduce(s32[]{:T(128)} %reduce_sum.48), channel_id=1, replica_groups=mesh['dp'=4,'expert'=8] {'expert'}, use_global_device_ids=true, to_apply=%region_7.9 | all-reduce | flops 1 | bytes 8 | tf_op jit(solution)/shard_map/psum | solution.py:47
  25.3 0.8 fusion.17
  26.1 0.7 compare_select_fusion.2
  27.0 1.1 concatenate.7
  28.1 0.9 gather_fusion.1
  29.0 0.8 multiply_convert_fusion
  29.9 3.4 %all-to-all-start.1 = ((bf16[8,16,896]{2,1,0:T(8,128)(2,1)}), bf16[8,16,896]{2,1,0:T(8,128)(2,1)S(1)}, u32[]{:S(2)}, u32[]{:S(2)}) async-start(bf16[8,16,896]{2,1,0:T(8,128)(2,1)} %bitcast.6), calls=%async_computation.1 | async-start | bytes 458752 | tf_op jit(solution)/shard_map/all_to_all | solution.py:64
  33.3 0.9 gather_fusion
  34.2 0.8 broadcast_select_fusion
  35.0 6.2 %all-to-all-done.1 = bf16[8,16,896]{2,1,0:T(8,128)(2,1)S(1)} async-done(((bf16[8,16,896]{2,1,0:T(8,128)(2,1)}), bf16[8,16,896]{2,1,0:T(8,128)(2,1)S(1)}, u32[]{:S(2)}, u32[]{:S(2)}) %all-to-all-start.1) | async-done | bytes 229408 | tf_op jit(solution)/shard_map/all_to_all | solution.py:64
  41.2 3.4 %all-to-all-start = ((bf16[8,16,896]{2,1,0:T(8,128)(2,1)}), bf16[8,16,896]{2,1,0:T(8,128)(2,1)S(1)}, u32[]{:S(2)}, u32[]{:S(2)}) async-start(bf16[8,16,896]{2,1,0:T(8,128)(2,1)} %bitcast.4), calls=%async_computation | async-start | bytes 458752 | tf_op jit(solution)/shard_map/all_to_all | solution.py:63
  44.7 9.3 %all_gather.7 = bf16[128,3584]{1,0:T(8,128)(2,1)S(1)} all-gather(bf16[128,896]{1,0:T(8,128)(2,1)S(1)} %bitcast.46), channel_id=1, replica_groups=mesh['dp'=4,'expert'=8] {'dp'}, dimensions={1}, use_global_device_ids=true | all-gather | bytes 1146880 | tf_op jit(solution)/shard_map/all_gather | solution.py:68
  54.0 9.4 %all_gather.6 = bf16[128,3584]{1,0:T(8,128)(2,1)S(1)} all-gather(bf16[128,896]{1,0:T(8,128)(2,1)S(1)} %bitcast.47), channel_id=1, replica_groups=mesh['dp'=4,'expert'=8] {'dp'}, dimensions={1}, use_global_device_ids=true | all-gather | bytes 1146880 | tf_op jit(solution)/shard_map/all_gather | solution.py:67
  63.4 0.4 fusion.8
  63.8 1.6 %multiply_convert_fusion.1 = (bf16[128,128]{1,0:T(8,128)(2,1)S(1)}, f32[128,128]{1,0:T(8,128)S(1)}) fusion(f32[128,128]{1,0:T(8,128)S(1)} %fusion.8, bf16[128,3584]{1,0:T(8,128)(2,1)S(1)} %all_gather.7, bf16[1,128,3584]{2,1,0:T(8,128)(2,1)} %param.17), kind=kOutput, calls=%fused_computation.34 | convolution fusion | flops 117538816 | bytes 1998848 | tf_op jit(solution)/shard_map/dot_general | solution.py:76
  65.4 0.4 fusion.5
  65.8 0.4 fusion.6
  66.2 0.4 fusion.3
  66.6 1.3 %copy.21 = bf16[3584,128]{1,0:T(8,128)(2,1)} copy(bf16[3584,128]{0,1:T(8,128)(2,1)S(1)} %fusion.3) | data formatting | bytes 1835008
  67.9 24.5 %reduce-scatter.4.cloned.1.call-done = bf16[896,128]{1,0:T(8,128)(2,1)} async-done(((bf16[3584,128]{1,0:T(8,128)(2,1)}), bf16[896,128]{1,0:T(8,128)(2,1)}) %reduce-scatter.4.cloned.1.call-update) | async-done | bytes 229392
  92.4 1.8 %copy.22 = bf16[896,128]{0,1:T(8,128)(2,1)} copy(bf16[896,128]{1,0:T(8,128)(2,1)} %reduce-scatter.4.cloned.1.call-done) | data formatting | bytes 458752
  94.2 5.5 %all-to-all-start.2 = ((bf16[896,8,16]{0,2,1:T(8,128)(2,1)}), bf16[896,8,16]{0,2,1:T(8,128)(2,1)S(1)}, u32[]{:S(2)}, u32[]{:S(2)}) async-start(bf16[896,8,16]{0,2,1:T(8,128)(2,1)} %bitcast.14), calls=%async_computation.2 | async-start | bytes 458752 | tf_op jit(solution)/shard_map/all_to_all | solution.py:92
  99.7 1.4 %fusion.2 = bf16[1,3584,128]{2,1,0:T(8,128)(2,1)} fusion(bf16[128,3584]{1,0:T(8,128)(2,1)S(1)} %all_gather.6, bf16[128,128]{1,0:T(8,128)(2,1)S(1)} %get-tuple-element.4), kind=kOutput, calls=%fused_computation.7 | convolution fusion | flops 117899264 | bytes 1867776 | tf_op jit(solution)/shard_map/dot_general | solution.py:84
  101.1 1.4 %fusion.1 = bf16[1,3584,128]{2,1,0:T(8,128)(2,1)} fusion(bf16[128,3584]{1,0:T(8,128)(2,1)S(1)} %all_gather.6, bf16[128,128]{1,0:T(8,128)(2,1)S(1)} %fusion.5), kind=kOutput, calls=%fused_computation.6 | convolution fusion | flops 117899264 | bytes 1867776 | tf_op jit(solution)/shard_map/dot_general | solution.py:81
  102.4 5.5 %all-to-all-done.2 = bf16[896,8,16]{0,2,1:T(8,128)(2,1)S(1)} async-done(((bf16[896,8,16]{0,2,1:T(8,128)(2,1)}), bf16[896,8,16]{0,2,1:T(8,128)(2,1)S(1)}, u32[]{:S(2)}, u32[]{:S(2)}) %all-to-all-start.2) | async-done | bytes 229408 | tf_op jit(solution)/shard_map/all_to_all | solution.py:92
  108.0 1.2 %convolution_convert_fusion.2 = bf16[256,896]{1,0:T(8,128)(2,1)} fusion(bf16[896,128]{0,1:T(8,128)(2,1)S(1)} %bitcast.45, s32[128]{0:T(128)S(1)} %select_n.37), kind=kOutput, calls=%fused_computation.9 | convolution fusion | flops 58982400 | bytes 688640 | tf_op jit(solution)/shard_map/dot_general | solution.py:98
  (23 shorter events, 0.5 us)
Async XLA Ops:
  7.2 56.2 %copy-start = (bf16[1,3584,128]{2,1,0:T(8,128)(2,1)S(1)}, bf16[1,3584,128]{2,1,0:T(8,128)(2,1)}, u32[]{:S(2)}) copy-start(bf16[1,3584,128]{2,1,0:T(8,128)(2,1)} %param.15) | copy-start | bytes 2752516
  27.0 6.2 %copy-start.2 = (bf16[256,896]{1,0:T(8,128)(2,1)S(1)}, bf16[256,896]{1,0:T(8,128)(2,1)}, u32[]{:S(2)}) copy-start(bf16[256,896]{1,0:T(8,128)(2,1)} %param.10) | copy-start | bytes 1376260
  29.9 11.3 %all-to-all-start.1 = ((bf16[8,16,896]{2,1,0:T(8,128)(2,1)}), bf16[8,16,896]{2,1,0:T(8,128)(2,1)S(1)}, u32[]{:S(2)}, u32[]{:S(2)}) async-start(bf16[8,16,896]{2,1,0:T(8,128)(2,1)} %bitcast.6), calls=%async_computation.1 | async-start | bytes 458752 | tf_op jit(solution)/shard_map/all_to_all | solution.py:64
  41.2 12.8 %all-to-all-start = ((bf16[8,16,896]{2,1,0:T(8,128)(2,1)}), bf16[8,16,896]{2,1,0:T(8,128)(2,1)S(1)}, u32[]{:S(2)}, u32[]{:S(2)}) async-start(bf16[8,16,896]{2,1,0:T(8,128)(2,1)} %bitcast.4), calls=%async_computation | async-start | bytes 458752 | tf_op jit(solution)/shard_map/all_to_all | solution.py:63
  44.6 47.8 %reduce-scatter.4.cloned.1.call-start = ((), (), s32[]{:S(2)}) async-start(), calls=%async_computation.4 | async-start | bytes 1146880
  63.4 2.0 %copy-start.1 = (bf16[1,3584,128]{2,1,0:T(8,128)(2,1)S(1)}, bf16[1,3584,128]{2,1,0:T(8,128)(2,1)}, u32[]{:S(2)}) copy-start(bf16[1,3584,128]{2,1,0:T(8,128)(2,1)} %param.16) | copy-start | bytes 2752516
  94.2 13.8 %all-to-all-start.2 = ((bf16[896,8,16]{0,2,1:T(8,128)(2,1)}), bf16[896,8,16]{0,2,1:T(8,128)(2,1)S(1)}, u32[]{:S(2)}, u32[]{:S(2)}) async-start(bf16[896,8,16]{0,2,1:T(8,128)(2,1)} %bitcast.14), calls=%async_computation.2 | async-start | bytes 458752 | tf_op jit(solution)/shard_map/all_to_all | solution.py:92
Sparse Core Ops, SparseCore 0:
  68.0 24.3 reduce-scatter.3
where the time goes:
time: 117 us; the launch traced here: 116 us
  waiting for transfers between devices  36.3 us (31%)
  blocking collectives  32.4 us (28%)
  between operations  14.9 us (13%)
  starting transfers between devices  12.4 us (11%)
  matrix products  7.07 us (6%)
  other arithmetic  6.57 us (6%)
  local copies, waits for them, and re-layouts  6.35 us (5%)
    unnamed x2, waiting for transfers between devices  24.5 us
    psum x1, blocking collectives, on_device(): forget_total = lax.psum(jnp.sum(forget_flags), 'expert')  13.7 us
    all_gather x1, blocking collectives, on_device(): lax.all_gather(part_tokens, 'dp', axis=1, tiled=True)  9.41 us
    all_gather x1, blocking collectives, on_device(): lax.all_gather(part_grads, 'dp', axis=1, tiled=True)  9.31 us
    all_to_all x1, waiting for transfers between devices, on_device(): lax.all_to_all(send_grads, 'expert', split_axis=0, concat_axis=0, tiled=T...  6.21 us
    all_to_all x1, waiting for transfers between devices, on_device(): lax.all_to_all(summed.astype(jnp.bfloat16), 'expert', split_axis=1, conca...  5.54 us
    all_to_all x1, starting transfers between devices, on_device(): lax.all_to_all(summed.astype(jnp.bfloat16), 'expert', split_axis=1, conca...  5.53 us
    all_to_all x1, starting transfers between devices, on_device(): lax.all_to_all(send_tokens, 'expert', split_axis=0, concat_axis=0, tiled=...  3.4 us
  transfers between devices with their start and end apart: 4, of which 3 were waited for; matrix products, arithmetic and copies ran while one was open for 4% of the time, Pallas kernels for 0%

commit v1 on v0

--- a/solution.py
+++ b/solution.py
@@ -41,6 +41,18 @@
 def on_device(
     tokens, token_grads, expert_ids, gate_values, forget_flags, gate_weight, up_weight, down_weight
 ):
+
+    def refer_copies(xin, dim_at, dim_no):
+        return jnp.concatenate(
+            jax.lax.all_to_all(
+                jnp.stack(jnp.split(xin, jax.lax.axis_size("expert"), axis=dim_at), axis=0),
+                "expert",
+                0,
+                0,
+            ),
+            axis=dim_no,
+        )
+
     n_dest = lax.axis_size("expert")
     row_count = tokens.shape[0]
     source, gate_sel, taken = slot_table(expert_ids, gate_values, CAP, n_dest)
@@ -89,9 +101,7 @@
     summed = lax.psum_scatter(
         (from_gate + from_up).astype(jnp.bfloat16), "dp", scatter_dimension=0, tiled=True
     ).astype(jnp.float32)
-    returned = lax.all_to_all(
-        summed.astype(jnp.bfloat16), "expert", split_axis=1, concat_axis=1, tiled=True
-    ).astype(summed.dtype)
+    returned = refer_copies(summed.astype(jnp.bfloat16), 1, 1).astype(summed.dtype)
     owner_match = (flat_source[:, None] == jnp.arange(row_count, dtype=jnp.int32)[None, :]).astype(
         jnp.float32
     )

time: 117 us -> 125 us (1.068)
  local copies, waits for them, and re-layouts: 6.35 us -> 14.6 us
    unnamed x8 -> x22, local copies, waits for them, and re-layouts: 3.05 us -> 7.51 us
    split x0 -> x1, local copies, waits for them, and re-layouts: none -> 3.17 us  [refer_copies(): jnp.split(xin, jax.lax.axis_size('expert'), axis=dim_at)]
where the time goes in v1:
time: 125 us; the launch traced here: 124 us
  waiting for transfers between devices  36.3 us (29%)
  blocking collectives  32.4 us (26%)
  between operations  14.9 us (12%)
  local copies, waits for them, and re-layouts  14.6 us (12%)
  starting transfers between devices  12.4 us (10%)
  matrix products  7.06 us (6%)
  other arithmetic  6.57 us (5%)
    unnamed x2, waiting for transfers between devices  24.5 us
    psum x1, blocking collectives, on_device(): forget_total = lax.psum(jnp.sum(forget_flags), 'expert')  13.7 us
    all_gather x1, blocking collectives, on_device(): lax.all_gather(part_tokens, 'dp', axis=1, tiled=True)  9.41 us
    all_gather x1, blocking collectives, on_device(): lax.all_gather(part_grads, 'dp', axis=1, tiled=True)  9.31 us
    unnamed x22, local copies, waits for them, and re-layouts  7.51 us
    all_to_all x1, waiting for transfers between devices, on_device(): lax.all_to_all(send_grads, 'expert', split_axis=0, concat_axis=0, tiled=T...  6.21 us
    all_to_all x1, waiting for transfers between devices, refer_copies(): jax.lax.all_to_all(jnp.stack(jnp.split(xin, jax.lax.axis_size('expert'),...  5.55 us
    all_to_all x1, starting transfers between devices, refer_copies(): jax.lax.all_to_all(jnp.stack(jnp.split(xin, jax.lax.axis_size('expert'),...  5.53 us
  transfers between devices with their start and end apart: 4, of which 3 were waited for; matrix products, arithmetic and copies ran while one was open for 4% of the time, Pallas kernels for 0%

profile of v1, /device:TPU:0, one launch (start us, length us, event | category | flops | bytes accessed | tf_op | source)
XLA Modules:
  0.0 124.2 jit_solution(10037323717572125247)
XLA Ops:
  7.2 0.9 fusion.16
  9.5 1.3 %reduce_sum.48 = s32[]{:T(128)} reduce(s32[256]{0:T(256)} %param.14, s32[]{:T(128)} %constant.4.clone.1), dimensions={0}, to_apply=%region_6.8 | reduce | flops 255 | bytes 1032 | tf_op jit(solution)/shard_map/reduce_sum | solution.py:59
  10.9 13.7 %psum.7 = s32[]{:T(128)} all-reduce(s32[]{:T(128)} %reduce_sum.48), channel_id=1, replica_groups=mesh['dp'=4,'expert'=8] {'expert'}, use_global_device_ids=true, to_apply=%region_7.9 | all-reduce | flops 1 | bytes 8 | tf_op jit(solution)/shard_map/psum | solution.py:59
  25.3 0.8 fusion.17
  26.1 0.7 compare_select_fusion.2
  27.0 1.1 concatenate.7
  28.1 0.9 gather_fusion.1
  29.0 0.8 multiply_convert_fusion
  29.9 3.4 %all-to-all-start.1 = ((bf16[8,16,896]{2,1,0:T(8,128)(2,1)}), bf16[8,16,896]{2,1,0:T(8,128)(2,1)S(1)}, u32[]{:S(2)}, u32[]{:S(2)}) async-start(bf16[8,16,896]{2,1,0:T(8,128)(2,1)} %bitcast.6), calls=%async_computation.1 | async-start | bytes 458752 | tf_op jit(solution)/shard_map/all_to_all | solution.py:76
  33.3 0.9 gather_fusion
  34.2 0.8 broadcast_select_fusion
  35.0 6.2 %all-to-all-done.1 = bf16[8,16,896]{2,1,0:T(8,128)(2,1)S(1)} async-done(((bf16[8,16,896]{2,1,0:T(8,128)(2,1)}), bf16[8,16,896]{2,1,0:T(8,128)(2,1)S(1)}, u32[]{:S(2)}, u32[]{:S(2)}) %all-to-all-start.1) | async-done | bytes 229408 | tf_op jit(solution)/shard_map/all_to_all | solution.py:76
  41.2 3.4 %all-to-all-start = ((bf16[8,16,896]{2,1,0:T(8,128)(2,1)}), bf16[8,16,896]{2,1,0:T(8,128)(2,1)S(1)}, u32[]{:S(2)}, u32[]{:S(2)}) async-start(bf16[8,16,896]{2,1,0:T(8,128)(2,1)} %bitcast.4), calls=%async_computation | async-start | bytes 458752 | tf_op jit(solution)/shard_map/all_to_all | solution.py:75
  44.7 9.3 %all_gather.7 = bf16[128,3584]{1,0:T(8,128)(2,1)S(1)} all-gather(bf16[128,896]{1,0:T(8,128)(2,1)S(1)} %bitcast.63), channel_id=1, replica_groups=mesh['dp'=4,'expert'=8] {'dp'}, dimensions={1}, use_global_device_ids=true | all-gather | bytes 1146880 | tf_op jit(solution)/shard_map/all_gather | solution.py:80
  54.0 9.4 %all_gather.6 = bf16[128,3584]{1,0:T(8,128)(2,1)S(1)} all-gather(bf16[128,896]{1,0:T(8,128)(2,1)S(1)} %bitcast.64), channel_id=1, replica_groups=mesh['dp'=4,'expert'=8] {'dp'}, dimensions={1}, use_global_device_ids=true | all-gather | bytes 1146880 | tf_op jit(solution)/shard_map/all_gather | solution.py:79
  63.8 1.6 %multiply_convert_fusion.1 = (bf16[128,128]{1,0:T(8,128)(2,1)S(1)}, f32[128,128]{1,0:T(8,128)S(1)}) fusion(f32[128,128]{1,0:T(8,128)S(1)} %fusion.8, bf16[128,3584]{1,0:T(8,128)(2,1)S(1)} %all_gather.7, bf16[1,128,3584]{2,1,0:T(8,128)(2,1)} %param.17), kind=kOutput, calls=%fused_computation.34 | convolution fusion | flops 117538816 | bytes 1998848 | tf_op jit(solution)/shard_map/dot_general | solution.py:88
  66.6 1.3 %copy.21 = bf16[3584,128]{1,0:T(8,128)(2,1)} copy(bf16[3584,128]{0,1:T(8,128)(2,1)S(1)} %fusion.3) | data formatting | bytes 1835008
  67.9 24.5 %reduce-scatter.4.cloned.1.call-done = bf16[896,128]{1,0:T(8,128)(2,1)} async-done(((bf16[3584,128]{1,0:T(8,128)(2,1)}), bf16[896,128]{1,0:T(8,128)(2,1)}) %reduce-scatter.4.cloned.1.call-update) | async-done | bytes 229392
  92.4 3.2 %fusion.19 = (bf16[896,16]{1,0:T(8,128)(2,1)S(1)}, bf16[896,16]{1,0:T(8,128)(2,1)S(1)}, bf16[896,16]{1,0:T(8,128)(2,1)S(1)}, bf16[896,16]{1,0:T(8,128)(2,1)S(1)}...) fusion(bf16[896,128]{1,0:T(8,128)(2,1)} %reduce-scatter.4.clone, ...), kind=kLoop, calls=%fused_computation.54 | loop fusion | bytes 458752 | tf_op jit(solution)/shard_map/split | solution.py:48
  95.6 1.0 copy.23
  96.6 0.6 bitcast_dynamic-update-slice_fusion.7
  98.1 0.6 bitcast_dynamic-update-slice_fusion.6
  98.8 0.6 bitcast_dynamic-update-slice_fusion.5
  99.4 0.6 bitcast_dynamic-update-slice_fusion.4
  100.0 0.6 bitcast_dynamic-update-slice_fusion.3
  100.6 0.6 bitcast_dynamic-update-slice_fusion.2
  101.8 0.6 bitcast_dynamic-update-slice_fusion
  102.4 5.5 %all-to-all-start.2 = ((bf16[8,896,16]{1,2,0:T(8,128)(2,1)}), bf16[8,896,16]{1,2,0:T(8,128)(2,1)S(1)}, u32[]{:S(2)}, u32[]{:S(2)}) async-start(bf16[8,896,16]{1,2,0:T(8,128)(2,1)} %bitcast_dynamic-update-slice_fusion), calls=%async_computation.2 | async-start | bytes 458752 | tf_op jit(solution)/shard_map/all_to_all | solution.py:47
  108.0 1.4 %fusion.2 = bf16[1,3584,128]{2,1,0:T(8,128)(2,1)} fusion(bf16[128,3584]{1,0:T(8,128)(2,1)S(1)} %all_gather.6, bf16[128,128]{1,0:T(8,128)(2,1)S(1)} %get-tuple-element.12), kind=kOutput, calls=%fused_computation.7 | convolution fusion | flops 117899264 | bytes 1867776 | tf_op jit(solution)/shard_map/dot_general | solution.py:96
  109.3 1.4 %fusion.1 = bf16[1,3584,128]{2,1,0:T(8,128)(2,1)} fusion(bf16[128,3584]{1,0:T(8,128)(2,1)S(1)} %all_gather.6, bf16[128,128]{1,0:T(8,128)(2,1)S(1)} %fusion.5), kind=kOutput, calls=%fused_computation.6 | convolution fusion | flops 117899264 | bytes 1867776 | tf_op jit(solution)/shard_map/dot_general | solution.py:93
  110.7 5.5 %all-to-all-done.2 = bf16[8,896,16]{1,2,0:T(8,128)(2,1)S(1)} async-done(((bf16[8,896,16]{1,2,0:T(8,128)(2,1)}), bf16[8,896,16]{1,2,0:T(8,128)(2,1)S(1)}, u32[]{:S(2)}, u32[]{:S(2)}) %all-to-all-start.2) | async-done | bytes 229408 | tf_op jit(solution)/shard_map/all_to_all | solution.py:47
  116.2 1.2 convolution_convert_fusion.2
  (39 shorter events, 4.9 us)
Async XLA Ops:
  7.2 56.2 %copy-start = (bf16[1,3584,128]{2,1,0:T(8,128)(2,1)S(1)}, bf16[1,3584,128]{2,1,0:T(8,128)(2,1)}, u32[]{:S(2)}) copy-start(bf16[1,3584,128]{2,1,0:T(8,128)(2,1)} %param.15) | copy-start | bytes 2752516
  27.0 6.2 %copy-start.2 = (bf16[256,896]{1,0:T(8,128)(2,1)S(1)}, bf16[256,896]{1,0:T(8,128)(2,1)}, u32[]{:S(2)}) copy-start(bf16[256,896]{1,0:T(8,128)(2,1)} %param.10) | copy-start | bytes 1376260
  29.9 11.3 %all-to-all-start.1 = ((bf16[8,16,896]{2,1,0:T(8,128)(2,1)}), bf16[8,16,896]{2,1,0:T(8,128)(2,1)S(1)}, u32[]{:S(2)}, u32[]{:S(2)}) async-start(bf16[8,16,896]{2,1,0:T(8,128)(2,1)} %bitcast.6), calls=%async_computation.1 | async-start | bytes 458752 | tf_op jit(solution)/shard_map/all_to_all | solution.py:76
  41.2 12.8 %all-to-all-start = ((bf16[8,16,896]{2,1,0:T(8,128)(2,1)}), bf16[8,16,896]{2,1,0:T(8,128)(2,1)S(1)}, u32[]{:S(2)}, u32[]{:S(2)}) async-start(bf16[8,16,896]{2,1,0:T(8,128)(2,1)} %bitcast.4), calls=%async_computation | async-start | bytes 458752 | tf_op jit(solution)/shard_map/all_to_all | solution.py:75
  44.6 47.8 %reduce-scatter.4.cloned.1.call-start = ((), (), s32[]{:S(2)}) async-start(), calls=%async_computation.4 | async-start | bytes 1146880
  63.4 2.0 %copy-start.1 = (bf16[1,3584,128]{2,1,0:T(8,128)(2,1)S(1)}, bf16[1,3584,128]{2,1,0:T(8,128)(2,1)}, u32[]{:S(2)}) copy-start(bf16[1,3584,128]{2,1,0:T(8,128)(2,1)} %param.16) | copy-start | bytes 2752516
  102.4 13.8 %all-to-all-start.2 = ((bf16[8,896,16]{1,2,0:T(8,128)(2,1)}), bf16[8,896,16]{1,2,0:T(8,128)(2,1)S(1)}, u32[]{:S(2)}, u32[]{:S(2)}) async-start(bf16[8,896,16]{1,2,0:T(8,128)(2,1)} %bitcast_dynamic-update-slice_fusion), calls=%async_computation.2 | async-start | bytes 458752 | tf_op jit(solution)/shard_map/all_to_all | solution.py:47
Sparse Core Ops, SparseCore 0:
  68.0 24.3 reduce-scatter.3
